TPU v7x, 256 devices: a whole 4x4x8 slice. The times are simulated.
256 devices in a mesh: grp: 8 (over x, core), cell: 32 (over y, z).
Axes of the slice: x: 4, y: 4, z: 8, core: 2. Of those that a mesh axis runs over, the one named last changes fastest.
Arguments:
- rhs: float32 [128, 2, 128, 16, 128], P('grp', None, 'cell'), may hold values from -8 to 8
- log_perm: float32 [128, 128, 16, 128], P('grp', 'cell'), may hold values from -1.5 to 1.5
- porosity: float32 [128, 128, 16, 128], P('grp', 'cell'), may hold values from 0.1 to 0.3
- saturation: float32 [128, 128, 16, 128], P('grp', 'cell'), may hold values from 0.2 to 0.8
- pressure: float32 [128, 128, 16, 128], P('grp', 'cell'), may hold values from -6 to 6
- obs_values: float32 [256], replicated, may hold values from -6 to 6
- obs_error: float32 [256], replicated, may hold values from 0.1 to 1
- noise: float32 [128, 256], replicated, may hold values from -6 to 6
- well_cell: int32 [128], replicated, may hold values from 0 to 262143
- obs_well: int32 [256], replicated, may hold values from 0 to 127
Outputs:
- increment: float32 [128, 2, 128, 16, 128], P('grp', None, 'cell')
- log_perm_post: float32 [128, 128, 16, 128], P('grp', 'cell')
- porosity_post: float32 [128, 128, 16, 128], P('grp', 'cell')
All inputs are finite; a program needn't handle non-finite values.
Results may differ from a plain program's by a relative error of at most 0.0003.
Values sent between devices are 32-bit elements; how exact they have to be, the bound alone decides.
No kernel may reach another device: no remote copies, remote signals or barrier semaphores. Data moves between devices by JAX's collectives and lax.ppermute only.
A program may use at most 128 MiB of HBM per device.

v0:
```python
import math
import jax
import jax.numpy as jnp
from jax import lax
from jax.sharding import Mesh
from jax.sharding import PartitionSpec as P

KRYLOV = 4
epsilon = 1e-06
time_step = 0.1
compress = 0.5
inflation = 4.0
CELL = ("cy", "cz")


def cell_sum(values, doubling=False):
    for axis in ("cz", "cy"):
        size = lax.axis_size(axis)
        if not doubling or size & size - 1:
            values = lax.psum(values, axis)
            continue
        step = 1
        while step < size:
            values = values + lax.ppermute(values, axis, [(i, i ^ step) for i in range(size)])
            step *= 2
    return values


def with_halo(block, sides, width):
    for axis, dim in sides:
        count = lax.axis_size(axis[0]) * lax.axis_size(axis[1])
        forward = [(i, i + 1) for i in range(count - 1)]
        backward = [(target, source) for source, target in forward]
        low = lax.ppermute(
            lax.slice_in_dim(block, block.shape[dim] - width, None, axis=dim), axis, forward
        )
        high = lax.ppermute(lax.slice_in_dim(block, 0, width, axis=dim), axis, backward)
        block = jnp.concatenate([low, block, high], axis=dim)
    return block


def mobility(sat_field):
    return sat_field * sat_field + 0.5 * (1.0 - sat_field) * (1.0 - sat_field)


def face_pair(perm_low, perm_high, sat_low, sat_high):
    trans = (
        2.0
        * perm_low
        * perm_high
        / (perm_low + perm_high)
        * (0.5 * (mobility(sat_low) + mobility(sat_high)))
    )
    return (trans, trans * (0.5 * (sat_low + sat_high)))


def plane_faces(perm, sat_field):
    plane_rows = perm.shape[-2]
    plane_cols = perm.shape[-1]
    keep_rows = (
        lax.broadcasted_iota(jnp.int32, (plane_rows, plane_cols), 0) < plane_rows - 1
    ).astype(jnp.float32)
    keep_cols = (
        lax.broadcasted_iota(jnp.int32, (plane_rows, plane_cols), 1) < plane_cols - 1
    ).astype(jnp.float32)
    trans_y, frac_y = face_pair(
        perm, jnp.roll(perm, -1, -2), sat_field, jnp.roll(sat_field, -1, -2)
    )
    trans_z, frac_z = face_pair(
        perm, jnp.roll(perm, -1, -1), sat_field, jnp.roll(sat_field, -1, -1)
    )
    return (trans_y * keep_rows, frac_y * keep_rows, trans_z * keep_cols, frac_z * keep_cols)


def operator(padded, second, coeffs):
    accum, trans_x, frac_x, trans_y, frac_y, trans_z, frac_z = coeffs
    first = padded[..., 1:-1, :, :]
    diff_x = padded[..., 1:, :, :] - padded[..., :-1, :, :]
    diff_y = jnp.roll(first, -1, -2) - first
    diff_z = jnp.roll(first, -1, -1) - first

    def net(coef_x, coef_y, coef_z):
        flow_x = coef_x * diff_x
        flow_y = coef_y * diff_y
        flow_z = coef_z * diff_z
        return (
            flow_x[..., :-1, :, :]
            - flow_x[..., 1:, :, :]
            + (jnp.roll(flow_y, 1, -2) - flow_y)
            + (jnp.roll(flow_z, 1, -1) - flow_z)
        )

    out_pressure = accum * (compress * first + 0.5 * second) + net(trans_x, trans_y, trans_z)
    out_water = accum * second + net(frac_x, frac_y, frac_z)
    return (out_pressure, out_water)


def least_squares(columns, beta):
    rows = [list(column) for column in columns]
    cosines = []
    sines = []
    target = [beta] + [jnp.zeros_like(beta) for column in columns]
    for jdx in range(len(rows)):
        column = rows[jdx]
        for idx in range(jdx):
            upper = cosines[idx] * column[idx] + sines[idx] * column[idx + 1]
            column[idx + 1] = -sines[idx] * column[idx] + cosines[idx] * column[idx + 1]
            column[idx] = upper
        radius = jnp.sqrt(column[jdx] * column[jdx] + column[jdx + 1] * column[jdx + 1])
        cosines.append(column[jdx] / radius)
        sines.append(column[jdx + 1] / radius)
        column[jdx] = radius
        target[jdx + 1] = -sines[jdx] * target[jdx]
        target[jdx] = cosines[jdx] * target[jdx]
    count = len(rows)
    solved = [None] * count
    for jdx in reversed(range(count)):
        partial_sum = target[jdx]
        for idx in range(jdx + 1, count):
            partial_sum = partial_sum - rows[idx][jdx] * solved[idx]
        solved[jdx] = partial_sum / rows[jdx][jdx]
    return solved


def ensemble_weights(predicted, obs_values, obs_error, noise, offset, count):
    members = predicted.shape[0]
    sigma = math.sqrt(inflation) * obs_error
    center = jnp.mean(predicted, axis=0)
    spread = (predicted - center) / (math.sqrt(members - 1.0) * sigma)
    innov = (obs_values + sigma * noise - predicted) / sigma
    own_innov = lax.dynamic_slice_in_dim(innov, offset, count, 0)
    gram = jnp.eye(members, dtype=jnp.float32) + jnp.dot(
        spread, spread.T, precision=lax.Precision.HIGHEST, preferred_element_type=jnp.float32
    )
    cross = jnp.dot(
        spread, own_innov.T, precision=lax.Precision.HIGHEST, preferred_element_type=jnp.float32
    )
    factor = jnp.linalg.cholesky(gram)
    return jax.scipy.linalg.cho_solve((factor, True), cross)


def expand(values):
    return values[:, None, None, None, None]


def inner(left, right):
    return jnp.sum(left * right, axis=(1, 2, 3, 4))


def local(
    rhs, log_perm, porosity, saturation, pressure, obs_values, obs_error, noise, well_cell, obs_well
):
    local_members, slab_x, plane_rows, plane_cols = log_perm.shape
    members = noise.shape[0]
    plane = plane_rows * plane_cols
    cells_dev = slab_x * plane
    slab_index = lax.axis_index("cy") * lax.axis_size("cz") + lax.axis_index("cz")
    slab_count = lax.axis_size("cy") * lax.axis_size("cz")
    count = slab_count
    forward = [(i, i + 1) for i in range(count - 1)]
    backward = [(target, source) for source, target in forward]
    edges = (log_perm, saturation, rhs[:, 0])
    low = lax.ppermute(jnp.stack([field[:, -1:] for field in edges], 1), CELL, forward)
    high = lax.ppermute(jnp.stack([field[:, :1] for field in edges], 1), CELL, backward)
    perm_pad = jnp.exp(jnp.concatenate([low[:, 0], log_perm, high[:, 0]], axis=1))
    sat_pad = jnp.concatenate([low[:, 1], saturation, high[:, 1]], axis=1)
    trans_x, frac_x = face_pair(perm_pad[:, :-1], perm_pad[:, 1:], sat_pad[:, :-1], sat_pad[:, 1:])
    face_pos = lax.broadcasted_iota(jnp.int32, (slab_x + 1, 1, 1), 0)
    keep_face = jnp.where(
        face_pos == 0,
        slab_index > 0,
        jnp.where(face_pos == slab_x, slab_index < slab_count - 1, True),
    ).astype(jnp.float32)
    trans_x = trans_x * keep_face
    frac_x = frac_x * keep_face
    trans_y, frac_y, trans_z, frac_z = plane_faces(perm_pad[:, 1:-1], saturation)
    coeffs = (porosity / time_step, trans_x, frac_x, trans_y, frac_y, trans_z, frac_z)

    def planes(field):
        low = lax.ppermute(field[:, -1:], CELL, forward)
        high = lax.ppermute(field[:, :1], CELL, backward)
        return (low, high)

    def apply(vector, ghosts):
        padded = jnp.concatenate([ghosts[0], vector[:, 0], ghosts[1]], axis=1)
        out_pressure, out_water = operator(padded, vector[:, 1], coeffs)
        return jnp.stack([out_pressure, out_water], 1)

    def scale_planes(ghosts, scale):
        factor = scale[:, None, None, None]
        return (ghosts[0] / factor, ghosts[1] / factor)

    rhs_planes = (low[:, 2], high[:, 2])
    image = apply(rhs, rhs_planes)
    image_planes = planes(image[:, 0])
    reduced = cell_sum(jnp.stack([inner(rhs, rhs), inner(rhs, image)], 0))
    beta = jnp.sqrt(reduced[0] + epsilon)
    basis = [rhs / expand(beta)]
    basis_planes = [scale_planes(rhs_planes, beta)]
    image = image / expand(beta)
    image_planes = scale_planes(image_planes, beta)
    projected = [reduced[1] / (beta * beta)]
    columns = []
    for jdx in range(KRYLOV):
        ortho = image
        ortho_low, ortho_high = image_planes
        for idx in range(jdx + 1):
            ortho = ortho - expand(projected[idx]) * basis[idx]
            factor = projected[idx][:, None, None, None]
            ortho_low = ortho_low - factor * basis_planes[idx][0]
            ortho_high = ortho_high - factor * basis_planes[idx][1]
        ortho_planes = (ortho_low, ortho_high)
        if jdx == KRYLOV - 1:
            height = jnp.sqrt(cell_sum(inner(ortho, ortho)) + epsilon)
            columns.append(projected + [height])
            break
        image = apply(ortho, ortho_planes)
        image_planes = planes(image[:, 0])
        parts = [inner(ortho, ortho)]
        parts += [inner(basis[idx], image) for idx in range(jdx + 1)]
        parts.append(inner(ortho, image))
        reduced = cell_sum(jnp.stack(parts, 0))
        height = jnp.sqrt(reduced[0] + epsilon)
        columns.append(projected + [height])
        basis.append(ortho / expand(height))
        basis_planes.append(scale_planes(ortho_planes, height))
        image = image / expand(height)
        image_planes = scale_planes(image_planes, height)
        projected = [reduced[1 + idx] / height for idx in range(jdx + 1)]
        projected.append(reduced[jdx + 2] / (height * height))
    solved = least_squares(columns, beta)
    increment = expand(solved[0]) * basis[0]
    for jdx in range(1, KRYLOV):
        increment = increment + expand(solved[jdx]) * basis[jdx]
    cells = jnp.take(well_cell, obs_well)
    wells = well_cell.shape[0]
    component = (jnp.arange(obs_well.shape[0], dtype=jnp.int32) >= wells).astype(jnp.int32)
    slab_row = cells // plane - slab_index * slab_x
    inside = (slab_row >= 0) & (slab_row < slab_x)
    rows = 2 * slab_x * plane_rows
    row = component * (slab_x * plane_rows) + slab_row * plane_rows + cells % plane // plane_cols
    col_z = cells % plane_cols
    state = jnp.stack([pressure + increment[:, 0], saturation + increment[:, 1]], 1)
    table = state.reshape(local_members * rows, plane_cols)
    pick_z = lax.broadcasted_iota(jnp.int32, (plane_cols, cells.shape[0]), 0) == col_z[None, :]
    by_row = jnp.dot(
        table,
        pick_z.astype(jnp.float32),
        precision=lax.Precision.HIGHEST,
        preferred_element_type=jnp.float32,
    )
    pick_row = (
        lax.broadcasted_iota(jnp.int32, (rows, cells.shape[0]), 0) == row[None, :]
    ) & inside[None, :]
    picked = jnp.sum(
        by_row.reshape(local_members, rows, cells.shape[0]) * pick_row.astype(jnp.float32)[None],
        axis=1,
    )
    slab_pred = cell_sum(picked, doubling=True)
    predicted = lax.all_gather(slab_pred, "grp", axis=0, tiled=True)
    params = jnp.stack([log_perm, porosity], 1).reshape(local_members, 2 * cells_dev)
    offset = lax.axis_index("grp") * local_members
    own_columns = ensemble_weights(predicted, obs_values, obs_error, noise, offset, local_members)
    scale_factor = 1.0 / math.sqrt(members - 1.0)
    scaled = params * scale_factor
    update = jnp.dot(
        own_columns.T,
        lax.all_gather(scaled, "grp", axis=0, tiled=True),
        precision=lax.Precision.HIGHEST,
        preferred_element_type=jnp.float32,
    )
    posterior = params + update
    posterior = posterior.reshape(local_members, 2, slab_x, plane_rows, plane_cols)
    return (increment, posterior[:, 0], posterior[:, 1])


def split_mesh(mesh):
    devices = mesh.devices
    groups, slabs = devices.shape
    along_z = len({device.coords[2] for device in devices[0]})
    return Mesh(devices.reshape(groups, slabs // along_z, along_z), ("grp", "cy", "cz"))


def solution(mesh):
    mesh = split_mesh(mesh)
    in_specs = (
        P("grp", None, CELL, None, None),
        P("grp", CELL, None, None),
        P("grp", CELL, None, None),
        P("grp", CELL, None, None),
        P("grp", CELL, None, None),
        P(),
        P(),
        P(),
        P(),
        P(),
    )
    out_specs = (
        P("grp", None, CELL, None, None),
        P("grp", CELL, None, None),
        P("grp", CELL, None, None),
    )
    return jax.shard_map(local, mesh=mesh, in_specs=in_specs, out_specs=out_specs, check_vma=False)
```

profile of v0, /device:TPU:1, one launch (start us, length us, event | category | flops | bytes accessed | tf_op | source)
XLA Modules:
  0.0 307.5 jit_solution(6333934453051698767)
XLA Ops:
  13.3 5.0 %collective-permute-start = (f32[16,3,1,16,128]{4,3,0,2,1:T(8,128)}, f32[16,3,1,16,128]{4,3,0,2,1:T(8,128)S(1)}, u32[]{:S(2)}, u32[]{:S(2)}) collective-permute-start(f32[16,3,1,16,128]{4,3,0,2,1:T(8,128)} %pad_maximum_fusion.12), channel_id=1, source_target_pairs={{0,1},{1,2},{2,3},{3,4},{4,5},{5,6},{6,7},{7,8},{8,9},{9,10},{10,1... | collective-permute-start | bytes 1179656 | tf_op jit(solution)/shard_map/ppermute | solution.py:163
  34.1 19.3 %psum.70 = f32[2,16]{1,0:T(2,128)S(1)} all-reduce(f32[2,16]{1,0:T(2,128)S(1)} %pad_maximum_fusion.16), channel_id=1, replica_groups=mesh['grp'=8,'cy'=4,'cz'=8] {'cz'}, use_global_device_ids=true, to_apply=%region_2.3 | all-reduce | flops 32 | bytes 256 | tf_op jit(solution)/shard_map/psum | solution.py:20
  53.5 10.3 %psum.71 = f32[2,16]{1,0:T(2,128)S(1)} all-reduce(f32[2,16]{1,0:T(2,128)S(1)} %psum.70), channel_id=1, replica_groups=mesh['grp'=8,'cy'=4,'cz'=8] {'cy'}, use_global_device_ids=true, to_apply=%region_3.4 | all-reduce | flops 32 | bytes 256 | tf_op jit(solution)/shard_map/psum | solution.py:20
  65.8 4.0 %collective-permute-start.3 = (f32[16,1,16,128]{3,2,1,0:T(8,128)S(1)}, f32[16,1,16,128]{3,2,1,0:T(8,128)S(1)}, u32[]{:S(2)}, u32[]{:S(2)}) collective-permute-start(f32[16,1,16,128]{3,2,1,0:T(8,128)S(1)} %get-tuple-element.72), channel_id=1, source_target_pairs={{0,1},{1,2},{2,3},{3,4},{4,5},{5,6},{6,7},{7,8},{8,9},{9,10},{10,1... | collective-permute-start | bytes 393224 | tf_op jit(solution)/shard_map/ppermute | solution.py:180
  76.6 14.2 %psum.72 = f32[3,16]{1,0:T(4,128)S(1)} all-reduce(f32[3,16]{1,0:T(4,128)S(1)} %pad_maximum_fusion.14), channel_id=1, replica_groups=mesh['grp'=8,'cy'=4,'cz'=8] {'cz'}, use_global_device_ids=true, to_apply=%region_7.8 | all-reduce | flops 48 | bytes 384 | tf_op jit(solution)/shard_map/psum | solution.py:20
  90.9 6.0 %psum.73 = f32[3,16]{1,0:T(4,128)S(1)} all-reduce(f32[3,16]{1,0:T(4,128)S(1)} %psum.72), channel_id=1, replica_groups=mesh['grp'=8,'cy'=4,'cz'=8] {'cy'}, use_global_device_ids=true, to_apply=%region_8.9 | all-reduce | flops 48 | bytes 384 | tf_op jit(solution)/shard_map/psum | solution.py:20
  97.4 2.6 multiply_subtract_fusion.1
  101.7 4.2 %collective-permute-start.5 = (f32[16,1,16,128]{3,2,1,0:T(8,128)S(1)}, f32[16,1,16,128]{3,2,1,0:T(8,128)S(1)}, u32[]{:S(2)}, u32[]{:S(2)}) collective-permute-start(f32[16,1,16,128]{3,2,1,0:T(8,128)S(1)} %get-tuple-element.70), channel_id=1, source_target_pairs={{0,1},{1,2},{2,3},{3,4},{4,5},{5,6},{6,7},{7,8},{8,9},{9,10},{10,1... | collective-permute-start | bytes 393224 | tf_op jit(solution)/shard_map/ppermute | solution.py:180
  112.2 14.7 %psum.74 = f32[4,16]{1,0:T(4,128)} all-reduce(f32[4,16]{1,0:T(4,128)S(1)} %pad_maximum_fusion.15), channel_id=1, replica_groups=mesh['grp'=8,'cy'=4,'cz'=8] {'cz'}, use_global_device_ids=true, to_apply=%region_13.14 | all-reduce | flops 64 | bytes 512 | tf_op jit(solution)/shard_map/psum | solution.py:20
  126.9 7.4 %psum.75 = f32[4,16]{1,0:T(4,128)} all-reduce(f32[4,16]{1,0:T(4,128)} %psum.74), channel_id=1, replica_groups=mesh['grp'=8,'cy'=4,'cz'=8] {'cy'}, use_global_device_ids=true, to_apply=%region_14.15 | all-reduce | flops 64 | bytes 512 | tf_op jit(solution)/shard_map/psum | solution.py:20
  136.1 2.4 copy_subtract_fusion
  140.3 4.0 %collective-permute-start.7 = (f32[16,1,16,128]{3,2,1,0:T(8,128)S(1)}, f32[16,1,16,128]{3,2,1,0:T(8,128)S(1)}, u32[]{:S(2)}, u32[]{:S(2)}) collective-permute-start(f32[16,1,16,128]{3,2,1,0:T(8,128)S(1)} %get-tuple-element.68), channel_id=1, source_target_pairs={{0,1},{1,2},{2,3},{3,4},{4,5},{5,6},{6,7},{7,8},{8,9},{9,10},{10,1... | collective-permute-start | bytes 393224 | tf_op jit(solution)/shard_map/ppermute | solution.py:180
  149.6 14.1 %psum.76 = f32[5,16]{1,0:T(8,128)S(1)} all-reduce(f32[5,16]{1,0:T(8,128)S(1)} %stack.169), channel_id=1, replica_groups=mesh['grp'=8,'cy'=4,'cz'=8] {'cz'}, use_global_device_ids=true, to_apply=%region_20.21 | all-reduce | flops 80 | bytes 640 | tf_op jit(solution)/shard_map/psum | solution.py:20
  163.7 7.9 %psum.77 = f32[5,16]{1,0:T(8,128)S(1)} all-reduce(f32[5,16]{1,0:T(8,128)S(1)} %psum.76), channel_id=1, replica_groups=mesh['grp'=8,'cy'=4,'cz'=8] {'cy'}, use_global_device_ids=true, to_apply=%region_21.22 | all-reduce | flops 80 | bytes 640 | tf_op jit(solution)/shard_map/psum | solution.py:20
  174.0 12.3 %psum.78 = f32[16]{0:T(128)S(1)} all-reduce(f32[16]{0:T(128)S(1)} %multiply_reduce_fusion.1), channel_id=1, replica_groups=mesh['grp'=8,'cy'=4,'cz'=8] {'cz'}, use_global_device_ids=true, to_apply=%region_23.24 | all-reduce | flops 16 | bytes 128 | tf_op jit(solution)/shard_map/psum | solution.py:20
  186.3 6.1 %psum.79 = f32[16]{0:T(128)S(1)} all-reduce(f32[16]{0:T(128)S(1)} %psum.78), channel_id=1, replica_groups=mesh['grp'=8,'cy'=4,'cz'=8] {'cy'}, use_global_device_ids=true, to_apply=%region_24.25 | all-reduce | flops 16 | bytes 128 | tf_op jit(solution)/shard_map/psum | solution.py:20
  197.7 2.5 collective-permute-done.8
  200.1 3.5 %collective-permute-done.9 = f32[16,256]{1,0:T(8,128)S(1)} collective-permute-done((f32[16,256]{1,0:T(8,128)S(1)}, f32[16,256]{1,0:T(8,128)S(1)}, u32[]{:S(2)}, u32[]{:S(2)}) %collective-permute-start.9) | collective-permute-done | bytes 16416 | tf_op jit(solution)/shard_map/ppermute | solution.py:24
  205.9 4.4 %collective-permute-done.10 = f32[16,256]{1,0:T(8,128)S(1)} collective-permute-done((f32[16,256]{1,0:T(8,128)S(1)}, f32[16,256]{1,0:T(8,128)S(1)}, u32[]{:S(2)}, u32[]{:S(2)}) %collective-permute-start.10) | collective-permute-done | bytes 16416 | tf_op jit(solution)/shard_map/ppermute | solution.py:24
  213.8 3.2 %collective-permute-done.12 = f32[16,256]{1,0:T(8,128)S(1)} collective-permute-done((f32[16,256]{1,0:T(8,128)S(1)}, f32[16,256]{1,0:T(8,128)S(1)}, u32[]{:S(2)}, u32[]{:S(2)}) %collective-permute-start.12) | collective-permute-done | bytes 16416 | tf_op jit(solution)/shard_map/ppermute | solution.py:24
  217.0 50.4 %all_gather.6 = f32[128,256]{1,0:T(8,128)S(1)} all-gather(f32[16,256]{1,0:T(8,128)S(1)} %add.480), channel_id=1, replica_groups=mesh['grp'=8,'cy'=4,'cz'=8] {'grp'}, dimensions={0}, use_global_device_ids=true | all-gather | bytes 147456 | tf_op jit(solution)/shard_map/all_gather | solution.py:260
  267.9 11.7 %cholesky.17 = f32[128,128]{1,0:T(8,128)S(1)} custom-call(f32[128,128]{1,0:T(8,128)S(1)} %fusion.71), custom_call_target="Cholesky" | custom-call | tf_op jit(solution)/shard_map/jit(cholesky)/cholesky | solution.py:138
  280.9 9.8 %custom-call.10 = f32[1,128,128]{1,2,0:T(8,128)S(1)} custom-call(f32[1,128,128]{2,1,0:T(8,128)S(1)} %fusion.65), custom_call_target="InvertDiagBlocksLowerTriangular" | custom-call | tf_op jit(solution)/shard_map/jit(_cho_solve)/triangular_solve | solution.py:139
  292.3 7.1 %fusion = f32[2,8,128,128]{3,1,2,0:T(8,128)S(1)} fusion(f32[128,16]{1,0:T(8,128)S(1)} %fusion.66, f32[128,16384]{1,0:T(8,128)} %all-gather.2.cloned.1.call-done, f32[2,8,128,128]{3,2,1,0:T(8,128)S(1)} %bitcast.504), kind=kOutput, calls=%fused_computation.3 | convolution fusion | flops 402915328 | bytes 10493952 | tf_op jit(solution)/shard_map/dot_general | solution.py:266
  (265 shorter events, 65.0 us)
Async XLA Ops:
  7.2 285.1 %all-gather.2.cloned.1.call-start = ((), (), s32[]{:S(2)}) async-start(), calls=%async_computation | async-start | bytes 9437184 | tf_op jit(solution)/shard_map/all_gather | solution.py:268
  11.3 15.3 %collective-permute-start.1 = (f32[16,3,1,16,128]{4,3,0,2,1:T(8,128)}, f32[16,3,1,16,128]{4,3,0,2,1:T(8,128)S(1)}, u32[]{:S(2)}, u32[]{:S(2)}) collective-permute-start(f32[16,3,1,16,128]{4,3,0,2,1:T(8,128)} %pad_maximum_fusion.13), channel_id=1, source_target_pairs={{1,0},{2,1},{3,2},{4,3},{5,4},{6,5},{7,6},{8,7},{9,8},{10,9},{11,1... | collective-permute-start | bytes 1179656 | tf_op jit(solution)/shard_map/ppermute | solution.py:164
  13.3 13.3 %collective-permute-start = (f32[16,3,1,16,128]{4,3,0,2,1:T(8,128)}, f32[16,3,1,16,128]{4,3,0,2,1:T(8,128)S(1)}, u32[]{:S(2)}, u32[]{:S(2)}) collective-permute-start(f32[16,3,1,16,128]{4,3,0,2,1:T(8,128)} %pad_maximum_fusion.12), channel_id=1, source_target_pairs={{0,1},{1,2},{2,3},{3,4},{4,5},{5,6},{6,7},{7,8},{8,9},{9,10},{10,1... | collective-permute-start | bytes 1179656 | tf_op jit(solution)/shard_map/ppermute | solution.py:163
  25.8 80.1 %copy-start.43 = (f32[128]{0:T(128)}, f32[128]{0:T(128)S(1)}, u32[]{:S(2)}) copy-start(f32[128]{0:T(128)S(1)} %compare_convert_fusion) | copy-start | bytes 1540
  25.8 80.1 %copy-start.44 = (f32[16]{0:T(128)}, f32[16]{0:T(128)S(1)}, u32[]{:S(2)}) copy-start(f32[16]{0:T(128)S(1)} %compare_convert_fusion.1) | copy-start | bytes 196
  64.4 9.1 %collective-permute-start.2 = (f32[16,1,16,128]{3,2,1,0:T(8,128)S(1)}, f32[16,1,16,128]{3,2,1,0:T(8,128)S(1)}, u32[]{:S(2)}, u32[]{:S(2)}) collective-permute-start(f32[16,1,16,128]{3,2,1,0:T(8,128)S(1)} %get-tuple-element.71), channel_id=1, source_target_pairs={{1,0},{2,1},{3,2},{4,3},{5,4},{6,5},{7,6},{8,7},{9,8},{10,9},{11,1... | collective-permute-start | bytes 393224 | tf_op jit(solution)/shard_map/ppermute | solution.py:181
  65.8 7.7 %collective-permute-start.3 = (f32[16,1,16,128]{3,2,1,0:T(8,128)S(1)}, f32[16,1,16,128]{3,2,1,0:T(8,128)S(1)}, u32[]{:S(2)}, u32[]{:S(2)}) collective-permute-start(f32[16,1,16,128]{3,2,1,0:T(8,128)S(1)} %get-tuple-element.72), channel_id=1, source_target_pairs={{0,1},{1,2},{2,3},{3,4},{4,5},{5,6},{6,7},{7,8},{8,9},{9,10},{10,1... | collective-permute-start | bytes 393224 | tf_op jit(solution)/shard_map/ppermute | solution.py:180
  100.4 8.0 %collective-permute-start.4 = (f32[16,1,16,128]{3,2,1,0:T(8,128)S(1)}, f32[16,1,16,128]{3,2,1,0:T(8,128)S(1)}, u32[]{:S(2)}, u32[]{:S(2)}) collective-permute-start(f32[16,1,16,128]{3,2,1,0:T(8,128)S(1)} %get-tuple-element.69), channel_id=1, source_target_pairs={{1,0},{2,1},{3,2},{4,3},{5,4},{6,5},{7,6},{8,7},{9,8},{10,9},{11,1... | collective-permute-start | bytes 393224 | tf_op jit(solution)/shard_map/ppermute | solution.py:181
  101.7 6.7 %collective-permute-start.5 = (f32[16,1,16,128]{3,2,1,0:T(8,128)S(1)}, f32[16,1,16,128]{3,2,1,0:T(8,128)S(1)}, u32[]{:S(2)}, u32[]{:S(2)}) collective-permute-start(f32[16,1,16,128]{3,2,1,0:T(8,128)S(1)} %get-tuple-element.70), channel_id=1, source_target_pairs={{0,1},{1,2},{2,3},{3,4},{4,5},{5,6},{6,7},{7,8},{8,9},{9,10},{10,1... | collective-permute-start | bytes 393224 | tf_op jit(solution)/shard_map/ppermute | solution.py:180
  138.9 7.2 %collective-permute-start.6 = (f32[16,1,16,128]{3,2,1,0:T(8,128)S(1)}, f32[16,1,16,128]{3,2,1,0:T(8,128)S(1)}, u32[]{:S(2)}, u32[]{:S(2)}) collective-permute-start(f32[16,1,16,128]{3,2,1,0:T(8,128)S(1)} %get-tuple-element.67), channel_id=1, source_target_pairs={{1,0},{2,1},{3,2},{4,3},{5,4},{6,5},{7,6},{8,7},{9,8},{10,9},{11,1... | collective-permute-start | bytes 393224 | tf_op jit(solution)/shard_map/ppermute | solution.py:181
  140.3 5.9 %collective-permute-start.7 = (f32[16,1,16,128]{3,2,1,0:T(8,128)S(1)}, f32[16,1,16,128]{3,2,1,0:T(8,128)S(1)}, u32[]{:S(2)}, u32[]{:S(2)}) collective-permute-start(f32[16,1,16,128]{3,2,1,0:T(8,128)S(1)} %get-tuple-element.68), channel_id=1, source_target_pairs={{0,1},{1,2},{2,3},{3,4},{4,5},{5,6},{6,7},{7,8},{8,9},{9,10},{10,1... | collective-permute-start | bytes 393224 | tf_op jit(solution)/shard_map/ppermute | solution.py:180
  148.2 44.2 %copy-start.42 = (f32[4,16]{1,0:T(4,128)S(1)}, f32[4,16]{1,0:T(4,128)}, u32[]{:S(2)}) copy-start(f32[4,16]{1,0:T(4,128)} %psum.75) | copy-start | bytes 772
  148.2 44.2 %copy-start.46 = (f32[3,16]{1,0:T(4,128)S(1)}, f32[3,16]{1,0:T(4,128)}, u32[]{:S(2)}) copy-start(f32[3,16]{1,0:T(4,128)} %copy-done.45) | copy-start | bytes 580
  148.2 44.2 %copy-start.48 = (f32[2,16]{1,0:T(2,128)S(1)}, f32[2,16]{1,0:T(2,128)}, u32[]{:S(2)}) copy-start(f32[2,16]{1,0:T(2,128)} %copy-done.47) | copy-start | bytes 388
  148.2 44.2 %copy-start.50 = (f32[16]{0:T(128)S(1)}, f32[16]{0:T(128)}, u32[]{:S(2)}) copy-start(f32[16]{0:T(128)} %copy-done.49) | copy-start | bytes 196
  148.2 44.2 %copy-start.52 = (f32[16]{0:T(128)S(1)}, f32[16]{0:T(128)}, u32[]{:S(2)}) copy-start(f32[16]{0:T(128)} %copy-done.51) | copy-start | bytes 196
  148.2 44.2 %copy-start.55 = (f32[16]{0:T(128)S(1)}, f32[16]{0:T(128)}, u32[]{:S(2)}) copy-start(f32[16]{0:T(128)} %get-tuple-element.97) | copy-start | bytes 196
  174.0 116.8 %copy-start.57 = (f32[256]{0:T(256)S(1)}, f32[256]{0:T(256)}, u32[]{:S(2)}) copy-start(f32[256]{0:T(256)} %param.15) | copy-start | bytes 3076
  194.6 97.7 %copy-start.24 = (f32[16,2,4,16,128]{4,3,2,1,0:T(8,128)S(1)}, f32[16,2,4,16,128]{4,3,2,1,0:T(8,128)}, u32[]{:S(2)}) copy-start(f32[16,2,4,16,128]{4,3,2,1,0:T(8,128)} %copy-done.23) | copy-start | bytes 3145732
  197.5 2.7 collective-permute-start.8
  200.1 3.5 %collective-permute-start.9 = (f32[16,256]{1,0:T(8,128)S(1)}, f32[16,256]{1,0:T(8,128)S(1)}, u32[]{:S(2)}, u32[]{:S(2)}) collective-permute-start(f32[16,256]{1,0:T(8,128)S(1)} %add.476), channel_id=1, source_target_pairs={{0,2},{1,3},{2,0},{3,1},{4,6},{5,7},{6,4},{7,5},{8,10},{9,11},{10,... | collective-permute-start | bytes 49160 | tf_op jit(solution)/shard_map/ppermute | solution.py:24
  203.7 6.7 %collective-permute-start.10 = (f32[16,256]{1,0:T(8,128)S(1)}, f32[16,256]{1,0:T(8,128)S(1)}, u32[]{:S(2)}, u32[]{:S(2)}) collective-permute-start(f32[16,256]{1,0:T(8,128)S(1)} %add.477), channel_id=1, source_target_pairs={{0,4},{1,5},{2,6},{3,7},{4,0},{5,1},{6,2},{7,3},{8,12},{9,13},{10,... | collective-permute-start | bytes 49160 | tf_op jit(solution)/shard_map/ppermute | solution.py:24
  210.3 2.6 collective-permute-start.11
  212.9 4.1 %collective-permute-start.12 = (f32[16,256]{1,0:T(8,128)S(1)}, f32[16,256]{1,0:T(8,128)S(1)}, u32[]{:S(2)}, u32[]{:S(2)}) collective-permute-start(f32[16,256]{1,0:T(8,128)S(1)} %add.479), channel_id=1, source_target_pairs={{0,16},{8,24},{16,0},{24,8},{1,17},{9,25},{17,1},{25,9},{2,18},{10... | collective-permute-start | bytes 49160 | tf_op jit(solution)/shard_map/ppermute | solution.py:24
  (48 other events, 515.4 us)
Sparse Core Ops, SparseCore 0:
  22.6 56.6 all-gather.1
where the time goes:
time: 308 us
  blocking collectives  163 us (53%)
  other arithmetic  64.7 us (21%)
  starting transfers between devices  27.4 us (9%)
  between operations  15.4 us (5%)
  waiting for transfers between devices  15 us (5%)
  local copies, waits for them, and re-layouts  12.4 us (4%)
  matrix products  9.87 us (3%)
    psum x10, blocking collectives, cell_sum(): values = lax.psum(values, axis)  112 us
    all_gather x1, blocking collectives, local(): predicted = lax.all_gather(slab_pred, 'grp', axis=0, tiled=True)  50.4 us
    ppermute x5, waiting for transfers between devices, cell_sum(): lax.ppermute(values, axis, [(i, i ^ step) for i in range(size)])  14.8 us
    another operation x3, other arithmetic, ensemble_weights(): factor = jnp.linalg.cholesky(gram)  12.4 us
    ppermute x3, starting transfers between devices, planes(): low = lax.ppermute(field[:, -1:], CELL, forward)  12.2 us
    another operation x2, other arithmetic, ensemble_weights(): return jax.scipy.linalg.cho_solve((factor, True), cross)  10.5 us
    mul x5, other arithmetic, net(): flow_z = coef_z * diff_z  7.78 us
    dot_general x1, matrix products, local(): jnp.dot(own_columns.T, lax.all_gather(scaled, 'grp', axis=0, tiled=True),...  7.11 us
  transfers between devices with their start and end apart: 14, of which 6 were waited for; matrix products, arithmetic and copies ran while one was open for 24% of the time, Pallas kernels for 0%

commit v1 on v0

--- a/solution.py
+++ b/solution.py
@@ -257,7 +257,11 @@
         axis=1,
     )
     slab_pred = cell_sum(picked, doubling=True)
-    predicted = lax.all_gather(slab_pred, "grp", axis=0, tiled=True)
+    n = jax.lax.axis_size("grp")
+    windows = [n if dev_i == 0 else 1 for dev_i in range(slab_pred.ndim)]
+    predicted = jax.lax.all_to_all(
+        jnp.tile(slab_pred, windows), "grp", split_axis=0, concat_axis=0, tiled=True
+    )
     params = jnp.stack([log_perm, porosity], 1).reshape(local_members, 2 * cells_dev)
     offset = lax.axis_index("grp") * local_members
     own_columns = ensemble_weights(predicted, obs_values, obs_error, noise, offset, local_members)

time: 308 us -> 306 us (level)
  blocking collectives: 163 us -> 112 us
  starting transfers between devices: 27.4 us -> 69.1 us
  waiting for transfers between devices: 15 us -> 20.2 us
    all_gather x1 -> x0, blocking collectives: 50.4 us -> none  [local(): predicted = lax.all_gather(slab_pred, 'grp', axis=0, tiled=True)]
    all_to_all x0 -> x1, starting transfers between devices: none -> 41.8 us  [local(): jax.lax.all_to_all(jnp.tile(slab_pred, windows), 'grp', split_axis=0, con...]
    all_to_all x0 -> x1, waiting for transfers between devices: none -> 5.23 us  [local(): jax.lax.all_to_all(jnp.tile(slab_pred, windows), 'grp', split_axis=0, con...]
  transfers between devices with their start and end apart: 14 -> 15, of which waited for: 6 -> 7; matrix products, arithmetic and copies ran while one was open for 24% -> 24% of each run, Pallas kernels for 0% -> 0%
where the time goes in v1:
time: 306 us; the launch traced here: 305 us
  blocking collectives  112 us (37%)
  starting transfers between devices  69.1 us (23%)
  other arithmetic  64.8 us (21%)
  waiting for transfers between devices  20.2 us (7%)
  between operations  15.5 us (5%)
  local copies, waits for them, and re-layouts  13.1 us (4%)
  matrix products  9.87 us (3%)
    psum x10, blocking collectives, cell_sum(): values = lax.psum(values, axis)  112 us
    all_to_all x1, starting transfers between devices, local(): jax.lax.all_to_all(jnp.tile(slab_pred, windows), 'grp', split_axis=0, con...  41.8 us
    ppermute x5, waiting for transfers between devices, cell_sum(): lax.ppermute(values, axis, [(i, i ^ step) for i in range(size)])  14.8 us
    another operation x3, other arithmetic, ensemble_weights(): factor = jnp.linalg.cholesky(gram)  12.4 us
    ppermute x3, starting transfers between devices, planes(): low = lax.ppermute(field[:, -1:], CELL, forward)  12.2 us
    another operation x2, other arithmetic, ensemble_weights(): return jax.scipy.linalg.cho_solve((factor, True), cross)  10.5 us
    mul x5, other arithmetic, net(): flow_z = coef_z * diff_z  7.76 us
    dot_general x1, matrix products, local(): jnp.dot(own_columns.T, lax.all_gather(scaled, 'grp', axis=0, tiled=True),...  7.11 us
  transfers between devices with their start and end apart: 15, of which 7 were waited for; matrix products, arithmetic and copies ran while one was open for 24% of the time, Pallas kernels for 0%

profile of v1, /device:TPU:1, one launch (start us, length us, event | category | flops | bytes accessed | tf_op | source)
XLA Modules:
  0.0 305.0 jit_solution(15206556631355171594)
XLA Ops:
  13.3 5.0 %collective-permute-start = (f32[16,3,1,16,128]{4,3,0,2,1:T(8,128)}, f32[16,3,1,16,128]{4,3,0,2,1:T(8,128)S(1)}, u32[]{:S(2)}, u32[]{:S(2)}) collective-permute-start(f32[16,3,1,16,128]{4,3,0,2,1:T(8,128)} %pad_maximum_fusion.12), channel_id=1, source_target_pairs={{0,1},{1,2},{2,3},{3,4},{4,5},{5,6},{6,7},{7,8},{8,9},{9,10},{10,1... | collective-permute-start | bytes 1179656 | tf_op jit(solution)/shard_map/ppermute | solution.py:163
  34.2 19.3 %psum.70 = f32[2,16]{1,0:T(2,128)S(1)} all-reduce(f32[2,16]{1,0:T(2,128)S(1)} %pad_maximum_fusion.16), channel_id=1, replica_groups=mesh['grp'=8,'cy'=4,'cz'=8] {'cz'}, use_global_device_ids=true, to_apply=%region_2.3 | all-reduce | flops 32 | bytes 256 | tf_op jit(solution)/shard_map/psum | solution.py:20
  53.5 10.2 %psum.71 = f32[2,16]{1,0:T(2,128)S(1)} all-reduce(f32[2,16]{1,0:T(2,128)S(1)} %psum.70), channel_id=1, replica_groups=mesh['grp'=8,'cy'=4,'cz'=8] {'cy'}, use_global_device_ids=true, to_apply=%region_3.4 | all-reduce | flops 32 | bytes 256 | tf_op jit(solution)/shard_map/psum | solution.py:20
  65.8 4.0 %collective-permute-start.3 = (f32[16,1,16,128]{3,2,1,0:T(8,128)S(1)}, f32[16,1,16,128]{3,2,1,0:T(8,128)S(1)}, u32[]{:S(2)}, u32[]{:S(2)}) collective-permute-start(f32[16,1,16,128]{3,2,1,0:T(8,128)S(1)} %get-tuple-element.72), channel_id=1, source_target_pairs={{0,1},{1,2},{2,3},{3,4},{4,5},{5,6},{6,7},{7,8},{8,9},{9,10},{10,1... | collective-permute-start | bytes 393224 | tf_op jit(solution)/shard_map/ppermute | solution.py:180
  76.6 14.2 %psum.72 = f32[3,16]{1,0:T(4,128)S(1)} all-reduce(f32[3,16]{1,0:T(4,128)S(1)} %pad_maximum_fusion.14), channel_id=1, replica_groups=mesh['grp'=8,'cy'=4,'cz'=8] {'cz'}, use_global_device_ids=true, to_apply=%region_7.8 | all-reduce | flops 48 | bytes 384 | tf_op jit(solution)/shard_map/psum | solution.py:20
  90.9 6.0 %psum.73 = f32[3,16]{1,0:T(4,128)S(1)} all-reduce(f32[3,16]{1,0:T(4,128)S(1)} %psum.72), channel_id=1, replica_groups=mesh['grp'=8,'cy'=4,'cz'=8] {'cy'}, use_global_device_ids=true, to_apply=%region_8.9 | all-reduce | flops 48 | bytes 384 | tf_op jit(solution)/shard_map/psum | solution.py:20
  97.5 2.6 multiply_subtract_fusion.1
  101.7 4.2 %collective-permute-start.5 = (f32[16,1,16,128]{3,2,1,0:T(8,128)S(1)}, f32[16,1,16,128]{3,2,1,0:T(8,128)S(1)}, u32[]{:S(2)}, u32[]{:S(2)}) collective-permute-start(f32[16,1,16,128]{3,2,1,0:T(8,128)S(1)} %get-tuple-element.70), channel_id=1, source_target_pairs={{0,1},{1,2},{2,3},{3,4},{4,5},{5,6},{6,7},{7,8},{8,9},{9,10},{10,1... | collective-permute-start | bytes 393224 | tf_op jit(solution)/shard_map/ppermute | solution.py:180
  112.2 14.7 %psum.74 = f32[4,16]{1,0:T(4,128)} all-reduce(f32[4,16]{1,0:T(4,128)S(1)} %pad_maximum_fusion.15), channel_id=1, replica_groups=mesh['grp'=8,'cy'=4,'cz'=8] {'cz'}, use_global_device_ids=true, to_apply=%region_13.14 | all-reduce | flops 64 | bytes 512 | tf_op jit(solution)/shard_map/psum | solution.py:20
  127.0 7.5 %psum.75 = f32[4,16]{1,0:T(4,128)} all-reduce(f32[4,16]{1,0:T(4,128)} %psum.74), channel_id=1, replica_groups=mesh['grp'=8,'cy'=4,'cz'=8] {'cy'}, use_global_device_ids=true, to_apply=%region_14.15 | all-reduce | flops 64 | bytes 512 | tf_op jit(solution)/shard_map/psum | solution.py:20
  140.4 4.0 %collective-permute-start.7 = (f32[16,1,16,128]{3,2,1,0:T(8,128)S(1)}, f32[16,1,16,128]{3,2,1,0:T(8,128)S(1)}, u32[]{:S(2)}, u32[]{:S(2)}) collective-permute-start(f32[16,1,16,128]{3,2,1,0:T(8,128)S(1)} %get-tuple-element.68), channel_id=1, source_target_pairs={{0,1},{1,2},{2,3},{3,4},{4,5},{5,6},{6,7},{7,8},{8,9},{9,10},{10,1... | collective-permute-start | bytes 393224 | tf_op jit(solution)/shard_map/ppermute | solution.py:180
  149.7 14.1 %psum.76 = f32[5,16]{1,0:T(8,128)S(1)} all-reduce(f32[5,16]{1,0:T(8,128)S(1)} %stack.169), channel_id=1, replica_groups=mesh['grp'=8,'cy'=4,'cz'=8] {'cz'}, use_global_device_ids=true, to_apply=%region_20.21 | all-reduce | flops 80 | bytes 640 | tf_op jit(solution)/shard_map/psum | solution.py:20
  163.8 7.9 %psum.77 = f32[5,16]{1,0:T(8,128)S(1)} all-reduce(f32[5,16]{1,0:T(8,128)S(1)} %psum.76), channel_id=1, replica_groups=mesh['grp'=8,'cy'=4,'cz'=8] {'cy'}, use_global_device_ids=true, to_apply=%region_21.22 | all-reduce | flops 80 | bytes 640 | tf_op jit(solution)/shard_map/psum | solution.py:20
  174.1 12.3 %psum.78 = f32[16]{0:T(128)S(1)} all-reduce(f32[16]{0:T(128)S(1)} %multiply_reduce_fusion.1), channel_id=1, replica_groups=mesh['grp'=8,'cy'=4,'cz'=8] {'cz'}, use_global_device_ids=true, to_apply=%region_23.24 | all-reduce | flops 16 | bytes 128 | tf_op jit(solution)/shard_map/psum | solution.py:20
  186.4 6.1 %psum.79 = f32[16]{0:T(128)S(1)} all-reduce(f32[16]{0:T(128)S(1)} %psum.78), channel_id=1, replica_groups=mesh['grp'=8,'cy'=4,'cz'=8] {'cy'}, use_global_device_ids=true, to_apply=%region_24.25 | all-reduce | flops 16 | bytes 128 | tf_op jit(solution)/shard_map/psum | solution.py:20
  197.8 2.5 collective-permute-done.8
  200.3 3.5 %collective-permute-done.9 = f32[16,256]{1,0:T(8,128)S(1)} collective-permute-done((f32[16,256]{1,0:T(8,128)S(1)}, f32[16,256]{1,0:T(8,128)S(1)}, u32[]{:S(2)}, u32[]{:S(2)}) %collective-permute-start.9) | collective-permute-done | bytes 16416 | tf_op jit(solution)/shard_map/ppermute | solution.py:24
  206.1 4.4 %collective-permute-done.10 = f32[16,256]{1,0:T(8,128)S(1)} collective-permute-done((f32[16,256]{1,0:T(8,128)S(1)}, f32[16,256]{1,0:T(8,128)S(1)}, u32[]{:S(2)}, u32[]{:S(2)}) %collective-permute-start.10) | collective-permute-done | bytes 16416 | tf_op jit(solution)/shard_map/ppermute | solution.py:24
  214.0 3.2 %collective-permute-done.12 = f32[16,256]{1,0:T(8,128)S(1)} collective-permute-done((f32[16,256]{1,0:T(8,128)S(1)}, f32[16,256]{1,0:T(8,128)S(1)}, u32[]{:S(2)}, u32[]{:S(2)}) %collective-permute-start.12) | collective-permute-done | bytes 16416 | tf_op jit(solution)/shard_map/ppermute | solution.py:24
  217.8 41.8 %all-to-all-start = ((f32[8,16,256]{2,1,0:T(8,128)}), f32[8,16,256]{2,1,0:T(8,128)S(1)}, u32[]{:S(2)}, u32[]{:S(2)}) async-start(f32[8,16,256]{2,1,0:T(8,128)} %tile.2), calls=%async_computation | async-start | bytes 262144 | tf_op jit(solution)/shard_map/all_to_all | solution.py:262
  259.6 5.2 %all-to-all-done = f32[8,16,256]{2,1,0:T(8,128)S(1)} async-done(((f32[8,16,256]{2,1,0:T(8,128)}), f32[8,16,256]{2,1,0:T(8,128)S(1)}, u32[]{:S(2)}, u32[]{:S(2)}) %all-to-all-start) | async-done | bytes 131104 | tf_op jit(solution)/shard_map/all_to_all | solution.py:262
  265.3 11.7 %cholesky.17 = f32[128,128]{1,0:T(8,128)S(1)} custom-call(f32[128,128]{1,0:T(8,128)S(1)} %fusion.74), custom_call_target="Cholesky" | custom-call | tf_op jit(solution)/shard_map/jit(cholesky)/cholesky | solution.py:138
  278.4 9.8 %custom-call.10 = f32[1,128,128]{1,2,0:T(8,128)S(1)} custom-call(f32[1,128,128]{2,1,0:T(8,128)S(1)} %fusion.68), custom_call_target="InvertDiagBlocksLowerTriangular" | custom-call | tf_op jit(solution)/shard_map/jit(_cho_solve)/triangular_solve | solution.py:139
  289.7 7.1 %fusion = f32[2,8,128,128]{3,1,2,0:T(8,128)S(1)} fusion(f32[128,16]{1,0:T(8,128)S(1)} %fusion.69, f32[128,16384]{1,0:T(8,128)} %all-gather.2.cloned.1.call-done, f32[2,8,128,128]{3,2,1,0:T(8,128)S(1)} %bitcast.508), kind=kOutput, calls=%fused_computation.3 | convolution fusion | flops 402915328 | bytes 10493952 | tf_op jit(solution)/shard_map/dot_general | solution.py:270
  (268 shorter events, 68.3 us)
Async XLA Ops:
  7.2 282.5 %all-gather.2.cloned.1.call-start = ((), (), s32[]{:S(2)}) async-start(), calls=%async_computation.1 | async-start | bytes 9437184 | tf_op jit(solution)/shard_map/all_gather | solution.py:272
  11.3 15.3 %collective-permute-start.1 = (f32[16,3,1,16,128]{4,3,0,2,1:T(8,128)}, f32[16,3,1,16,128]{4,3,0,2,1:T(8,128)S(1)}, u32[]{:S(2)}, u32[]{:S(2)}) collective-permute-start(f32[16,3,1,16,128]{4,3,0,2,1:T(8,128)} %pad_maximum_fusion.13), channel_id=1, source_target_pairs={{1,0},{2,1},{3,2},{4,3},{5,4},{6,5},{7,6},{8,7},{9,8},{10,9},{11,1... | collective-permute-start | bytes 1179656 | tf_op jit(solution)/shard_map/ppermute | solution.py:164
  13.3 13.3 %collective-permute-start = (f32[16,3,1,16,128]{4,3,0,2,1:T(8,128)}, f32[16,3,1,16,128]{4,3,0,2,1:T(8,128)S(1)}, u32[]{:S(2)}, u32[]{:S(2)}) collective-permute-start(f32[16,3,1,16,128]{4,3,0,2,1:T(8,128)} %pad_maximum_fusion.12), channel_id=1, source_target_pairs={{0,1},{1,2},{2,3},{3,4},{4,5},{5,6},{6,7},{7,8},{8,9},{9,10},{10,1... | collective-permute-start | bytes 1179656 | tf_op jit(solution)/shard_map/ppermute | solution.py:163
  25.8 80.1 %copy-start.43 = (f32[128]{0:T(128)}, f32[128]{0:T(128)S(1)}, u32[]{:S(2)}) copy-start(f32[128]{0:T(128)S(1)} %compare_convert_fusion) | copy-start | bytes 1540
  25.8 80.1 %copy-start.44 = (f32[16]{0:T(128)}, f32[16]{0:T(128)S(1)}, u32[]{:S(2)}) copy-start(f32[16]{0:T(128)S(1)} %compare_convert_fusion.1) | copy-start | bytes 196
  64.4 9.1 %collective-permute-start.2 = (f32[16,1,16,128]{3,2,1,0:T(8,128)S(1)}, f32[16,1,16,128]{3,2,1,0:T(8,128)S(1)}, u32[]{:S(2)}, u32[]{:S(2)}) collective-permute-start(f32[16,1,16,128]{3,2,1,0:T(8,128)S(1)} %get-tuple-element.71), channel_id=1, source_target_pairs={{1,0},{2,1},{3,2},{4,3},{5,4},{6,5},{7,6},{8,7},{9,8},{10,9},{11,1... | collective-permute-start | bytes 393224 | tf_op jit(solution)/shard_map/ppermute | solution.py:181
  65.8 7.7 %collective-permute-start.3 = (f32[16,1,16,128]{3,2,1,0:T(8,128)S(1)}, f32[16,1,16,128]{3,2,1,0:T(8,128)S(1)}, u32[]{:S(2)}, u32[]{:S(2)}) collective-permute-start(f32[16,1,16,128]{3,2,1,0:T(8,128)S(1)} %get-tuple-element.72), channel_id=1, source_target_pairs={{0,1},{1,2},{2,3},{3,4},{4,5},{5,6},{6,7},{7,8},{8,9},{9,10},{10,1... | collective-permute-start | bytes 393224 | tf_op jit(solution)/shard_map/ppermute | solution.py:180
  100.4 8.0 %collective-permute-start.4 = (f32[16,1,16,128]{3,2,1,0:T(8,128)S(1)}, f32[16,1,16,128]{3,2,1,0:T(8,128)S(1)}, u32[]{:S(2)}, u32[]{:S(2)}) collective-permute-start(f32[16,1,16,128]{3,2,1,0:T(8,128)S(1)} %get-tuple-element.69), channel_id=1, source_target_pairs={{1,0},{2,1},{3,2},{4,3},{5,4},{6,5},{7,6},{8,7},{9,8},{10,9},{11,1... | collective-permute-start | bytes 393224 | tf_op jit(solution)/shard_map/ppermute | solution.py:181
  101.7 6.7 %collective-permute-start.5 = (f32[16,1,16,128]{3,2,1,0:T(8,128)S(1)}, f32[16,1,16,128]{3,2,1,0:T(8,128)S(1)}, u32[]{:S(2)}, u32[]{:S(2)}) collective-permute-start(f32[16,1,16,128]{3,2,1,0:T(8,128)S(1)} %get-tuple-element.70), channel_id=1, source_target_pairs={{0,1},{1,2},{2,3},{3,4},{4,5},{5,6},{6,7},{7,8},{8,9},{9,10},{10,1... | collective-permute-start | bytes 393224 | tf_op jit(solution)/shard_map/ppermute | solution.py:180
  139.0 7.2 %collective-permute-start.6 = (f32[16,1,16,128]{3,2,1,0:T(8,128)S(1)}, f32[16,1,16,128]{3,2,1,0:T(8,128)S(1)}, u32[]{:S(2)}, u32[]{:S(2)}) collective-permute-start(f32[16,1,16,128]{3,2,1,0:T(8,128)S(1)} %get-tuple-element.67), channel_id=1, source_target_pairs={{1,0},{2,1},{3,2},{4,3},{5,4},{6,5},{7,6},{8,7},{9,8},{10,9},{11,1... | collective-permute-start | bytes 393224 | tf_op jit(solution)/shard_map/ppermute | solution.py:181
  140.4 5.9 %collective-permute-start.7 = (f32[16,1,16,128]{3,2,1,0:T(8,128)S(1)}, f32[16,1,16,128]{3,2,1,0:T(8,128)S(1)}, u32[]{:S(2)}, u32[]{:S(2)}) collective-permute-start(f32[16,1,16,128]{3,2,1,0:T(8,128)S(1)} %get-tuple-element.68), channel_id=1, source_target_pairs={{0,1},{1,2},{2,3},{3,4},{4,5},{5,6},{6,7},{7,8},{8,9},{9,10},{10,1... | collective-permute-start | bytes 393224 | tf_op jit(solution)/shard_map/ppermute | solution.py:180
  148.3 44.2 %copy-start.42 = (f32[4,16]{1,0:T(4,128)S(1)}, f32[4,16]{1,0:T(4,128)}, u32[]{:S(2)}) copy-start(f32[4,16]{1,0:T(4,128)} %psum.75) | copy-start | bytes 772
  148.3 44.2 %copy-start.46 = (f32[3,16]{1,0:T(4,128)S(1)}, f32[3,16]{1,0:T(4,128)}, u32[]{:S(2)}) copy-start(f32[3,16]{1,0:T(4,128)} %copy-done.45) | copy-start | bytes 580
  148.3 44.2 %copy-start.48 = (f32[2,16]{1,0:T(2,128)S(1)}, f32[2,16]{1,0:T(2,128)}, u32[]{:S(2)}) copy-start(f32[2,16]{1,0:T(2,128)} %copy-done.47) | copy-start | bytes 388
  148.3 44.2 %copy-start.50 = (f32[16]{0:T(128)S(1)}, f32[16]{0:T(128)}, u32[]{:S(2)}) copy-start(f32[16]{0:T(128)} %copy-done.49) | copy-start | bytes 196
  174.1 85.5 %copy-start.56 = (f32[256]{0:T(256)S(1)}, f32[256]{0:T(256)}, u32[]{:S(2)}) copy-start(f32[256]{0:T(256)} %param.16) | copy-start | bytes 3076
  192.6 95.6 %copy-start.57 = (f32[256]{0:T(256)S(1)}, f32[256]{0:T(256)}, u32[]{:S(2)}) copy-start(f32[256]{0:T(256)} %param.15) | copy-start | bytes 3076
  194.7 95.0 %copy-start.24 = (f32[16,2,4,16,128]{4,3,2,1,0:T(8,128)S(1)}, f32[16,2,4,16,128]{4,3,2,1,0:T(8,128)}, u32[]{:S(2)}) copy-start(f32[16,2,4,16,128]{4,3,2,1,0:T(8,128)} %copy-done.23) | copy-start | bytes 3145732
  197.6 2.7 collective-permute-start.8
  200.3 3.5 %collective-permute-start.9 = (f32[16,256]{1,0:T(8,128)S(1)}, f32[16,256]{1,0:T(8,128)S(1)}, u32[]{:S(2)}, u32[]{:S(2)}) collective-permute-start(f32[16,256]{1,0:T(8,128)S(1)} %add.476), channel_id=1, source_target_pairs={{0,2},{1,3},{2,0},{3,1},{4,6},{5,7},{6,4},{7,5},{8,10},{9,11},{10,... | collective-permute-start | bytes 49160 | tf_op jit(solution)/shard_map/ppermute | solution.py:24
  203.8 6.7 %collective-permute-start.10 = (f32[16,256]{1,0:T(8,128)S(1)}, f32[16,256]{1,0:T(8,128)S(1)}, u32[]{:S(2)}, u32[]{:S(2)}) collective-permute-start(f32[16,256]{1,0:T(8,128)S(1)} %add.477), channel_id=1, source_target_pairs={{0,4},{1,5},{2,6},{3,7},{4,0},{5,1},{6,2},{7,3},{8,12},{9,13},{10,... | collective-permute-start | bytes 49160 | tf_op jit(solution)/shard_map/ppermute | solution.py:24
  210.5 2.6 collective-permute-start.11
  213.1 4.1 %collective-permute-start.12 = (f32[16,256]{1,0:T(8,128)S(1)}, f32[16,256]{1,0:T(8,128)S(1)}, u32[]{:S(2)}, u32[]{:S(2)}) collective-permute-start(f32[16,256]{1,0:T(8,128)S(1)} %add.479), channel_id=1, source_target_pairs={{0,16},{8,24},{16,0},{24,8},{1,17},{9,25},{17,1},{25,9},{2,18},{10... | collective-permute-start | bytes 49160 | tf_op jit(solution)/shard_map/ppermute | solution.py:24
  217.8 47.0 %all-to-all-start = ((f32[8,16,256]{2,1,0:T(8,128)}), f32[8,16,256]{2,1,0:T(8,128)S(1)}, u32[]{:S(2)}, u32[]{:S(2)}) async-start(f32[8,16,256]{2,1,0:T(8,128)} %tile.2), calls=%async_computation | async-start | bytes 262144 | tf_op jit(solution)/shard_map/all_to_all | solution.py:262
  (49 other events, 564.2 us)
Sparse Core Ops, SparseCore 0:
  22.6 56.6 all-gather.1
